TPU v7x, 256 devices: a whole 4x4x8 slice. The times are simulated.
256 devices in a mesh: dp: 32 (over z, y), tensor: 8 (over x, core).
Axes of the slice: x: 4, y: 4, z: 8, core: 2. Of those that a mesh axis runs over, the one named last changes fastest.
Arguments:
- tokens: bfloat16 [4096, 4096], P('dp', 'tensor'), may hold values from -6 to 6
- grad_out: bfloat16 [4096, 4096], P('dp', 'tensor'), may hold values from -6 to 6
- gate_blocks: int32 [8, 32], P('tensor'), may hold values from -1 to 447, as said below
- gate_values: bfloat16 [8, 32, 128, 128], P('tensor'), may hold values from -0.375 to 0.375
- up_blocks: int32 [8, 32], P('tensor'), may hold values from -1 to 447, as said below
- up_values: bfloat16 [8, 32, 128, 128], P('tensor'), may hold values from -0.375 to 0.375
- down_blocks: int32 [8, 32], P('tensor'), may hold values from -1 to 447, as said below
- down_values: bfloat16 [8, 32, 128, 128], P('tensor'), may hold values from -0.1875 to 0.1875
Outputs:
- mixed: bfloat16 [4096, 4096], P('dp', 'tensor')
- grad_tokens: bfloat16 [4096, 4096], P('dp', 'tensor')
- grad_gate: float32 [8, 32, 128, 128], P('tensor', 'dp')
- grad_up: float32 [8, 32, 128, 128], P('tensor', 'dp')
- grad_down: float32 [8, 32, 128, 128], P('tensor', 'dp')
Inputs may be any that keep to these rules, and one draw needn't show every extreme that they name: `gate_blocks`: each row lists distinct block numbers of one tensor shard in its first slots and -1 in the rest; a row has 16 to 32 listed blocks, one row has exactly 32 and another exactly 16. `up_blocks`: as for gate_blocks, drawn apart. `down_blocks`: as for gate_blocks, drawn apart.
All inputs are finite; a program needn't handle non-finite values.
Results may differ from a plain program's by a relative error of at most 0.015.
Values may be sent and summed in bfloat16 or wider, within the bound.
No kernel may reach another device: no remote copies, remote signals or barrier semaphores. Data moves between devices by JAX's collectives and lax.ppermute only.
A program may use at most 64 MiB of HBM per device.

v0:
```python
import jax
import jax.numpy as jnp
from jax import lax
from jax.sharding import PartitionSpec as P

FF = 14336


def locate(blocks, feature_count):
    flat = blocks[0]
    weight = (flat >= 0).astype(jnp.float32)
    safe = jnp.maximum(flat, 0)
    return (safe // feature_count, safe % feature_count, weight)


def one_hot(targets, weight, count):
    return (targets[:, None] == jnp.arange(count)[None, :]).astype(jnp.float32) * weight[:, None]


def spread(product, table):
    return jnp.einsum("tsn,sc->tcn", product, table, precision=lax.Precision.HIGHEST)


def select(source, position):
    return jnp.take(source, position, axis=1)


def forward_blocks(rows_in, values):
    return jnp.einsum("tsk,skn->tsn", rows_in, values, preferred_element_type=jnp.float32)


def backward_blocks(rows_in, values):
    return jnp.einsum("tsn,skn->tsk", rows_in, values, preferred_element_type=jnp.float32)


def slot_term(left, right, weight):
    product = jnp.einsum("tsk,tsn->skn", left, right, preferred_element_type=jnp.float32)
    return product * weight[:, None, None]


def body(
    tokens, grad_out, gate_blocks, gate_values, up_blocks, up_values, down_blocks, down_values
):
    gathered_x, gathered_dy = (
        lax.all_gather(tokens, "tensor", axis=1, tiled=True),
        lax.all_gather(grad_out, "tensor", axis=1, tiled=True),
    )
    tok_rows, feature_width = gathered_x.shape
    block_size = gate_values.shape[-1]
    feature_count = feature_width // block_size
    hidden_count = FF // (block_size * lax.axis_size("tensor"))
    inputs = gathered_x.reshape(tok_rows, feature_count, block_size)
    upstream = gathered_dy.reshape(tok_rows, feature_count, block_size)
    gate_hid, gate_feat, gate_live = locate(gate_blocks, feature_count)
    up_hid, up_feat, up_live = locate(up_blocks, feature_count)
    down_hid, down_feat, down_live = locate(down_blocks, feature_count)
    gate_rows = select(inputs, gate_feat)
    up_rows = select(inputs, up_feat)
    gate_pre = spread(
        forward_blocks(gate_rows, gate_values[0]), one_hot(gate_hid, gate_live, hidden_count)
    )
    up_pre = spread(forward_blocks(up_rows, up_values[0]), one_hot(up_hid, up_live, hidden_count))
    sigma_gate = jax.nn.sigmoid(gate_pre)
    activated = gate_pre * sigma_gate
    hidden = (activated * up_pre).astype(jnp.bfloat16)
    hidden_rows = select(hidden, down_hid)
    mixed_part = spread(
        forward_blocks(hidden_rows, down_values[0]), one_hot(down_feat, down_live, feature_count)
    )
    mixed_part = mixed_part.reshape(tok_rows, feature_width)
    upstream_rows = select(upstream, down_feat)
    mixed = lax.psum_scatter(
        mixed_part.astype(jnp.bfloat16), "tensor", scatter_dimension=1, tiled=True
    )
    hidden_grad = spread(
        backward_blocks(upstream_rows, down_values[0]), one_hot(down_hid, down_live, hidden_count)
    )
    gate_delta = (hidden_grad * up_pre * sigma_gate * (1.0 + gate_pre * (1.0 - sigma_gate))).astype(
        jnp.bfloat16
    )
    up_delta = (hidden_grad * activated).astype(jnp.bfloat16)
    gate_delta_rows = select(gate_delta, gate_hid)
    up_delta_rows = select(up_delta, up_hid)
    input_part = spread(
        backward_blocks(gate_delta_rows, gate_values[0]),
        one_hot(gate_feat, gate_live, feature_count),
    )
    input_part = input_part + spread(
        backward_blocks(up_delta_rows, up_values[0]), one_hot(up_feat, up_live, feature_count)
    )
    input_part = input_part.reshape(tok_rows, feature_width)
    gate_term = slot_term(gate_rows, gate_delta_rows, gate_live)
    up_term = slot_term(up_rows, up_delta_rows, up_live)
    down_term = slot_term(hidden_rows, upstream_rows, down_live)
    combined = lax.psum_scatter(
        jnp.stack([gate_term, up_term, down_term], axis=1).astype(jnp.bfloat16),
        "dp",
        scatter_dimension=0,
        tiled=True,
    ).astype(jnp.float32)
    grad_gate = combined[None, :, 0]
    grad_up = combined[None, :, 1]
    grad_down = combined[None, :, 2]
    grad_tokens = lax.psum_scatter(
        input_part.astype(jnp.bfloat16), "tensor", scatter_dimension=1, tiled=True
    )
    return (mixed, grad_tokens, grad_gate, grad_up, grad_down)


def solution(mesh):
    in_specs = (
        P("dp", "tensor"),
        P("dp", "tensor"),
        P("tensor", None),
        P("tensor", None, None, None),
        P("tensor", None),
        P("tensor", None, None, None),
        P("tensor", None),
        P("tensor", None, None, None),
    )
    out_specs = (
        P("dp", "tensor"),
        P("dp", "tensor"),
        P("tensor", "dp", None, None),
        P("tensor", "dp", None, None),
        P("tensor", "dp", None, None),
    )
    return jax.shard_map(body, mesh=mesh, in_specs=in_specs, out_specs=out_specs, check_vma=False)
```

profile of v0, /device:TPU:8, one launch (start us, length us, event | category | flops | bytes accessed | tf_op | source)
XLA Modules:
  0.0 338.6 jit_solution(3957242304848105937)
XLA Ops:
  7.2 0.0 copy-start
  7.2 0.0 all-gather.3.cloned.1.call-start
  7.2 1.7 copy.68
  9.0 0.0 all-gather.3.cloned.1.call-update
  9.0 0.0 all-gather.5.cloned.1.call-start
  9.0 1.7 copy.76
  10.7 0.0 all-gather.5.cloned.1.call-update
  10.7 0.0 all-reduce.3.cloned.1.call-start
  10.8 0.7 compare_and_fusion.1
  11.5 0.7 compare_and_fusion
  12.2 0.7 compare_and_fusion.2
  13.0 0.7 fusion.81
  13.6 0.7 fusion.82
  14.3 0.7 fusion.80
  14.9 24.2 %all-gather.3.cloned.1.call-done = bf16[128,4096]{0,1:T(8,128)(2,1)} async-done(((bf16[128,512]{0,1:T(8,128)(2,1)}), bf16[128,4096]{0,1:T(8,128)(2,1)}) %all-gather.3.cloned.1.call-update) | async-done | bytes 1048592 | tf_op jit(solution)/shard_map/all_gather | solution.py:45
  39.1 1.6 copy.69
  40.7 1.7 gather_fusion
  42.4 1.7 gather_fusion.1
  44.0 23.2 %all-gather.5.cloned.1.call-done = bf16[128,4096]{0,1:T(8,128)(2,1)} async-done(((bf16[128,512]{0,1:T(8,128)(2,1)}), bf16[128,4096]{0,1:T(8,128)(2,1)}) %all-gather.5.cloned.1.call-update) | async-done | bytes 1048592 | tf_op jit(solution)/shard_map/all_gather | solution.py:46
  67.2 2.3 copy.77
  69.5 0.0 copy-done.7
  69.5 0.5 convolution_bitcast_fusion.5
  70.0 0.0 copy-start.5
  70.0 3.2 fusion.10
  73.2 0.5 convolution_bitcast_fusion.4
  73.7 0.0 copy-start.2
  73.8 3.3 fusion.8
  77.0 2.9 gather_fusion.3
  79.9 2.1 convolution_bitcast_fusion.2
  82.0 0.0 copy-start.8
  82.0 0.0 copy-start.9
  82.0 2.2 fusion.4
  84.3 1.1 fusion.40
  85.4 1.7 gather_fusion.4
  87.0 3.2 fusion.17
  90.2 1.7 gather_fusion.5
  91.9 3.2 fusion.18
  95.1 1.7 gather_fusion.2
  96.8 2.5 fusion.19
  99.4 0.0 copy-done.10
  99.4 0.0 copy-done.11
  99.4 2.0 pad_maximum_fusion
  101.4 0.0 all-reduce.3.cloned.1.call-update
  101.5 0.0 reduce-scatter.8.cloned.1.call-start
  101.5 2.2 convolution_bitcast_fusion
  103.7 0.9 convolution_bitcast_fusion.1
  104.6 3.0 fusion
  107.6 3.1 add_convert_fusion
  110.8 0.0 copy-start.3
  110.8 1.4 copy.123
  112.2 0.0 reduce-scatter.8.cloned.1.call-update
  112.2 0.3 reduce-scatter.6.cloned.1.call-start
  112.5 0.2 copy-done.4
  112.7 0.5 convolution_bitcast_fusion.3
  113.2 3.0 fusion.14
  116.2 0.0 copy-start.12
  116.2 1.5 copy.124
  117.7 0.0 reduce-scatter.6.cloned.1.call-update
  117.8 0.6 dynamic-slice
  118.4 140.7 %all-reduce.3.cloned.1.call-done = bf16[32,3,128,128]{3,2,0,1:T(8,128)(2,1)} async-done(((bf16[32,3,128,128]{3,2,0,1:T(8,128)(2,1)}), bf16[32,3,128,128]{3,2,0,1:T(8,128)(2,1)}) %all-reduce.3.cloned.1.call-update) | async-done | bytes 3145744
  259.0 1.6 dynamic-slice_convert_fusion
  260.6 0.7 slice_bitcast_fusion
  261.3 34.3 %reduce-scatter.8.cloned.1.call-done = bf16[128,512]{1,0:T(8,128)(2,1)} async-done(((bf16[128,4096]{1,0:T(8,128)(2,1)}), bf16[128,512]{1,0:T(8,128)(2,1)}) %reduce-scatter.8.cloned.1.call-update) | async-done | bytes 131088 | tf_op jit(solution)/shard_map/reduce_scatter | solution.py:104
  295.5 36.6 %reduce-scatter.6.cloned.1.call-done = bf16[128,512]{1,0:T(8,128)(2,1)} async-done(((bf16[128,4096]{1,0:T(8,128)(2,1)}), bf16[128,512]{1,0:T(8,128)(2,1)}) %reduce-scatter.6.cloned.1.call-update) | async-done | bytes 131088 | tf_op jit(solution)/shard_map/reduce_scatter | solution.py:72
  (27 shorter events, 0.1 us)
Async XLA Ops:
  7.2 66.1 %copy-start = (bf16[1,32,128,128]{3,2,1,0:T(8,128)(2,1)S(1)}, bf16[1,32,128,128]{3,2,1,0:T(8,128)(2,1)}, u32[]{:S(2)}) copy-start(bf16[1,32,128,128]{3,2,1,0:T(8,128)(2,1)} %param.17) | copy-start | bytes 3145732
  7.2 31.9 %all-gather.3.cloned.1.call-start = ((), (), s32[]{:S(2)}) async-start(), calls=%async_computation.2 | async-start | bytes 1179648 | tf_op jit(solution)/shard_map/all_gather | solution.py:45
  9.0 58.3 %all-gather.5.cloned.1.call-start = ((), (), s32[]{:S(2)}) async-start(), calls=%async_computation.4 | async-start | bytes 1179648 | tf_op jit(solution)/shard_map/all_gather | solution.py:46
  10.7 248.3 %all-reduce.3.cloned.1.call-start = ((), (), s32[]{:S(2)}) async-start(), calls=%async_computation.6 | async-start | bytes 6291456
  42.4 27.1 %copy-start.1 = (bf16[1,32,128,128]{3,2,1,0:T(8,128)(2,1)S(1)}, bf16[1,32,128,128]{3,2,1,0:T(8,128)(2,1)}, u32[]{:S(2)}) copy-start(bf16[1,32,128,128]{3,2,1,0:T(8,128)(2,1)} %param.15) | copy-start | bytes 3145732
  44.0 25.5 %copy-start.7 = (bf16[32,128,128]{2,1,0:T(8,128)(2,1)S(1)}, bf16[32,128,128]{2,1,0:T(8,128)(2,1)}, u32[]{:S(2)}) copy-start(bf16[32,128,128]{2,1,0:T(8,128)(2,1)} %gather_fusion) | copy-start | bytes 3145732
  70.0 3.2 copy-start.5
  73.7 6.2 %copy-start.2 = (bf16[1,32,128,128]{3,2,1,0:T(8,128)(2,1)S(1)}, bf16[1,32,128,128]{3,2,1,0:T(8,128)(2,1)}, u32[]{:S(2)}) copy-start(bf16[1,32,128,128]{3,2,1,0:T(8,128)(2,1)} %param.19) | copy-start | bytes 3145732
  82.0 2.3 copy-start.8
  82.0 2.3 copy-start.9
  96.8 2.5 copy-start.10
  96.8 2.6 copy-start.11
  101.5 2.3 copy-start.6
  101.5 194.1 %reduce-scatter.8.cloned.1.call-start = ((), (), s32[]{:S(2)}) async-start(), calls=%async_computation.5 | async-start | bytes 1179648 | tf_op jit(solution)/shard_map/reduce_scatter | solution.py:104
  110.8 1.7 copy-start.3
  110.8 1.9 copy-start.4
  112.2 219.9 %reduce-scatter.6.cloned.1.call-start = ((), (), s32[]{:S(2)}) async-start(), calls=%async_computation.3 | async-start | bytes 1179648 | tf_op jit(solution)/shard_map/reduce_scatter | solution.py:72
  116.2 1.5 copy-start.12
Sparse Core Ops, SparseCore 0:
  10.4 28.6 all-gather.2
  41.5 25.6 all-gather.4
  101.6 157.3 all-reduce.2
  262.0 33.5 reduce-scatter.7
  298.5 33.5 reduce-scatter.5
where the time goes:
time: 339 us
  waiting for transfers between devices  259 us (76%)
  matrix products  33.4 us (10%)
  local copies, waits for them, and re-layouts  23 us (7%)
  between operations  14.1 us (4%)
  other arithmetic  8.69 us (3%)
    unnamed x6, waiting for transfers between devices  141 us
    reduce_scatter x1, waiting for transfers between devices, body(): lax.psum_scatter(mixed_part.astype(jnp.bfloat16), 'tensor', scatter_dimen...  36.6 us
    reduce_scatter x1, waiting for transfers between devices, body(): lax.psum_scatter(input_part.astype(jnp.bfloat16), 'tensor', scatter_dimen...  34.3 us
    all_gather x1, waiting for transfers between devices, body(): lax.all_gather(tokens, 'tensor', axis=1, tiled=True)  24.2 us
    all_gather x1, waiting for transfers between devices, body(): lax.all_gather(grad_out, 'tensor', axis=1, tiled=True)  23.2 us
    dot_general x6, matrix products, spread(): jnp.einsum('tsn,sc->tcn', product, table, precision=lax.Precision.HIGHEST)  17.9 us
    gather x6, local copies, waits for them, and re-layouts, select(): return jnp.take(source, position, axis=1)  11.3 us
    dot_general x3, matrix products, slot_term(): jnp.einsum('tsk,tsn->skn', left, right, preferred_element_type=jnp.float32)  8.89 us
  transfers between devices with their start and end apart: 5, of which 5 were waited for; matrix products, arithmetic and copies ran while one was open for 9% of the time, Pallas kernels for 0%

commit v1 on v0

--- a/solution.py
+++ b/solution.py
@@ -43,7 +43,9 @@
 ):
     gathered_x, gathered_dy = (
         lax.all_gather(tokens, "tensor", axis=1, tiled=True),
-        lax.all_gather(grad_out, "tensor", axis=1, tiled=True),
+        jnp.concatenate(
+            lax.all_to_all(jnp.stack([grad_out] * lax.axis_size("tensor")), "tensor", 0, 0), axis=1
+        ),
     )
     tok_rows, feature_width = gathered_x.shape
     block_size = gate_values.shape[-1]

time: 339 us -> 310 us (0.914)
  waiting for transfers between devices: 259 us -> 231 us
  starting transfers between devices: 0.43 us -> 4.68 us
  other arithmetic: 8.69 us -> 4.73 us
    all_gather x1, waiting for transfers between devices: 24.2 us -> 0.01 us  [body(): lax.all_gather(tokens, 'tensor', axis=1, tiled=True)]
    all_gather x1 -> x0, waiting for transfers between devices: 23.2 us -> none  [body(): lax.all_gather(grad_out, 'tensor', axis=1, tiled=True)]
    all_to_all x0 -> x1, waiting for transfers between devices: none -> 17.7 us  [body(): lax.all_to_all(jnp.stack([grad_out] * lax.axis_size('tensor')), 'tensor',...]
    all_to_all x0 -> x1, starting transfers between devices: none -> 4.3 us  [body(): lax.all_to_all(jnp.stack([grad_out] * lax.axis_size('tensor')), 'tensor',...]
    unnamed x6 -> x5, waiting for transfers between devices: 141 us -> 142 us
    unnamed x32 -> x36, local copies, waits for them, and re-layouts: 7.85 us -> 7.51 us
  transfers between devices with their start and end apart: 5 -> 5, of which waited for: 5 -> 4; matrix products, arithmetic and copies ran while one was open for 9% -> 9% of each run, Pallas kernels for 0% -> 0%
where the time goes in v1:
time: 310 us; the launch traced here: 309 us
  waiting for transfers between devices  231 us (75%)
  matrix products  32.1 us (10%)
  local copies, waits for them, and re-layouts  22.3 us (7%)
  between operations  14.2 us (5%)
  other arithmetic  4.73 us (2%)
  starting transfers between devices  4.68 us (2%)
    unnamed x5, waiting for transfers between devices  142 us
    reduce_scatter x1, waiting for transfers between devices, body(): lax.psum_scatter(mixed_part.astype(jnp.bfloat16), 'tensor', scatter_dimen...  36.6 us
    reduce_scatter x1, waiting for transfers between devices, body(): lax.psum_scatter(input_part.astype(jnp.bfloat16), 'tensor', scatter_dimen...  34.4 us
    all_to_all x1, waiting for transfers between devices, body(): lax.all_to_all(jnp.stack([grad_out] * lax.axis_size('tensor')), 'tensor',...  17.7 us
    dot_general x6, matrix products, spread(): jnp.einsum('tsn,sc->tcn', product, table, precision=lax.Precision.HIGHEST)  16.8 us
    gather x6, local copies, waits for them, and re-layouts, select(): return jnp.take(source, position, axis=1)  10.6 us
    dot_general x3, matrix products, slot_term(): jnp.einsum('tsk,tsn->skn', left, right, preferred_element_type=jnp.float32)  8.72 us
    unnamed x36, local copies, waits for them, and re-layouts  7.51 us
  transfers between devices with their start and end apart: 5, of which 4 were waited for; matrix products, arithmetic and copies ran while one was open for 9% of the time, Pallas kernels for 0%

profile of v1, /device:TPU:8, one launch (start us, length us, event | category | flops | bytes accessed | tf_op | source)
XLA Modules:
  0.0 309.2 jit_solution(8520456577807228322)
XLA Ops:
  7.2 0.0 copy-start
  7.2 0.0 copy-start.11
  7.2 0.0 copy-start.12
  7.2 0.0 copy-start.13
  7.2 0.0 all-gather.2.cloned.1.call-start
  7.3 1.7 copy.70
  9.0 0.0 all-gather.2.cloned.1.call-update
  9.0 1.0 copy.78
  10.0 1.1 stack.27
  11.2 4.3 %all-to-all-start = ((bf16[8,128,512]{1,2,0:T(8,128)(2,1)}), bf16[8,128,512]{1,2,0:T(8,128)(2,1)S(1)}, u32[]{:S(2)}, u32[]{:S(2)}) async-start(bf16[8,128,512]{1,2,0:T(8,128)(2,1)} %stack.27), calls=%async_computation.1 | async-start | bytes 2097152 | tf_op jit(solution)/shard_map/all_to_all | solution.py:47
  15.5 0.0 all-reduce.3.cloned.1.call-start
  15.5 0.0 copy-done.11
  15.6 0.0 copy-done.12
  15.7 0.0 copy-done.13
  15.8 17.7 %all-to-all-done = bf16[8,128,512]{1,2,0:T(8,128)(2,1)S(1)} async-done(((bf16[8,128,512]{1,2,0:T(8,128)(2,1)}), bf16[8,128,512]{1,2,0:T(8,128)(2,1)S(1)}, u32[]{:S(2)}, u32[]{:S(2)}) %all-to-all-start) | async-done | bytes 1048608 | tf_op jit(solution)/shard_map/all_to_all | solution.py:47
  33.5 1.3 copy.79
  34.8 2.0 gather_fusion.3
  36.8 0.0 copy-start.4
  36.8 0.0 copy-done.2
  36.8 0.9 convolution_bitcast_fusion.2
  37.7 0.1 copy-done.4
  37.8 3.2 %fusion.4 = f32[14,128,128]{2,0,1:T(8,128)} fusion(f32[128,32,128]{2,0,1:T(8,128)S(1)} %convolution_bitcast_fusion.2, f32[32]{0:T(128)S(1)} %fusion.80, s32[32]{0:T(128)S(1)} %get-tuple-element.51), kind=kOutput, calls=%fused_computation.11 | convolution fusion | flops 88081280 | bytes 3014912 | tf_op jit(solution)/shard_map/tsn,sc->tcn/dot_general | solution.py:21
  41.0 1.8 copy.71
  42.8 0.0 copy-start.1
  42.8 1.7 gather_fusion
  44.5 1.7 gather_fusion.1
  46.3 0.0 copy-done.1
  46.3 1.7 convolution_bitcast_fusion.5
  48.0 2.2 fusion.10
  50.3 0.5 convolution_bitcast_fusion.4
  50.8 0.0 copy-start.8
  50.8 2.2 fusion.8
  53.0 0.0 copy-done.8
  53.0 1.1 fusion.40
  54.1 1.7 gather_fusion.4
  55.7 3.2 %fusion.17 = bf16[32,1,128,128]{3,2,0,1:T(8,128)(2,1)} fusion(f32[32]{0:T(128)S(1)} %fusion.81, bf16[32,128,128]{2,1,0:T(8,128)(2,1)} %gather_fusion, pred[32]{0:T(512)(128)(4,1)S(1)} %get-tuple-element.52, bf16[32,128,128]{2,1,0:T(8,128)(2,1)} %gather_fusion.4, pred[32]{0:T(512)(128)(4,1)S(1)} %get-tuple-element.32), kind=kOutput, calls=%fused_computation.30 | convolution fusion | flops 136314880 | bytes 3145920 | tf_op jit(solution)/shard_map/tsk,tsn->skn/dot_general | solution.py:37
  58.9 1.8 gather_fusion.5
  60.7 3.2 %fusion.18 = bf16[32,1,128,128]{3,2,0,1:T(8,128)(2,1)} fusion(f32[32]{0:T(128)S(1)} %fusion.82, bf16[32,128,128]{2,1,0:T(8,128)(2,1)} %gather_fusion.1, pred[32]{0:T(512)(128)(4,1)S(1)} %get-tuple-element.54, bf16[32,128,128]{2,1,0:T(8,128)(2,1)} %gather_fusion.5, pred[32]{0:T(512)(128)(4,1)S(1)} %get-tuple-element.34), kind=kOutput, calls=%fused_computation.31 | convolution fusion | flops 136314880 | bytes 3145920 | tf_op jit(solution)/shard_map/tsk,tsn->skn/dot_general | solution.py:37
  63.9 1.7 gather_fusion.2
  65.6 2.4 fusion.19
  68.0 2.0 pad_maximum_fusion
  70.0 0.0 all-reduce.3.cloned.1.call-update
  70.0 0.3 reduce-scatter.8.cloned.1.call-start
  70.3 2.1 convolution_bitcast_fusion
  72.5 0.9 convolution_bitcast_fusion.1
  73.4 3.0 fusion
  76.4 3.1 %add_convert_fusion = bf16[32,128,128]{2,0,1:T(8,128)(2,1)S(1)} fusion(f32[32,128,128]{2,0,1:T(8,128)S(1)} %fusion, f32[128,32,128]{2,0,1:T(8,128)S(1)} %convolution_bitcast_fusion.1, f32[32]{0:T(128)S(1)} %fusion.81, s32[32]{0:T(128)S(1)} %get-tuple-element.53), kind=kOutput, calls=%fused_computation.22 | convolution fusion | flops 202377216 | bytes 5243136 | tf_op jit(solution)/shard_map/tsn,sc->tcn/dot_general | solution.py:21
  79.5 0.0 copy-start.3
  79.5 0.0 copy-start.5
  79.5 1.4 copy.125
  81.0 0.0 reduce-scatter.8.cloned.1.call-update
  81.0 0.0 reduce-scatter.6.cloned.1.call-start
  81.0 0.4 copy-done.5
  81.4 0.5 convolution_bitcast_fusion.3
  81.9 3.0 fusion.14
  84.9 0.0 copy-start.14
  84.9 1.5 copy.126
  86.5 0.0 reduce-scatter.6.cloned.1.call-update
  86.5 0.6 dynamic-slice
  87.1 142.3 %all-reduce.3.cloned.1.call-done = bf16[32,3,128,128]{3,2,0,1:T(8,128)(2,1)} async-done(((bf16[32,3,128,128]{3,2,0,1:T(8,128)(2,1)}), bf16[32,3,128,128]{3,2,0,1:T(8,128)(2,1)}) %all-reduce.3.cloned.1.call-update) | async-done | bytes 3145744
  229.4 1.6 dynamic-slice_convert_fusion
  231.0 0.7 slice_bitcast_fusion
  231.7 34.4 %reduce-scatter.8.cloned.1.call-done = bf16[128,512]{1,0:T(8,128)(2,1)} async-done(((bf16[128,4096]{1,0:T(8,128)(2,1)}), bf16[128,512]{1,0:T(8,128)(2,1)}) %reduce-scatter.8.cloned.1.call-update) | async-done | bytes 131088 | tf_op jit(solution)/shard_map/reduce_scatter | solution.py:106
  266.1 36.6 %reduce-scatter.6.cloned.1.call-done = bf16[128,512]{1,0:T(8,128)(2,1)} async-done(((bf16[128,4096]{1,0:T(8,128)(2,1)}), bf16[128,512]{1,0:T(8,128)(2,1)}) %reduce-scatter.6.cloned.1.call-update) | async-done | bytes 131088 | tf_op jit(solution)/shard_map/reduce_scatter | solution.py:74
  (31 shorter events, 0.1 us)
Async XLA Ops:
  7.2 43.1 %copy-start = (bf16[1,32,128,128]{3,2,1,0:T(8,128)(2,1)S(1)}, bf16[1,32,128,128]{3,2,1,0:T(8,128)(2,1)}, u32[]{:S(2)}) copy-start(bf16[1,32,128,128]{3,2,1,0:T(8,128)(2,1)} %param.17) | copy-start | bytes 3145732
  7.2 8.4 %copy-start.11 = (s32[1,32]{1,0:T(1,128)S(1)}, s32[1,32]{1,0:T(1,128)}, u32[]{:S(2)}) copy-start(s32[1,32]{1,0:T(1,128)} %param.14) | copy-start | bytes 388
  7.2 8.4 %copy-start.12 = (s32[1,32]{1,0:T(1,128)S(1)}, s32[1,32]{1,0:T(1,128)}, u32[]{:S(2)}) copy-start(s32[1,32]{1,0:T(1,128)} %param.16) | copy-start | bytes 388
  7.2 8.5 %copy-start.13 = (s32[1,32]{1,0:T(1,128)S(1)}, s32[1,32]{1,0:T(1,128)}, u32[]{:S(2)}) copy-start(s32[1,32]{1,0:T(1,128)} %param.18) | copy-start | bytes 388
  7.2 33.8 %all-gather.2.cloned.1.call-start = ((), (), s32[]{:S(2)}) async-start(), calls=%async_computation.3 | async-start | bytes 1179648 | tf_op jit(solution)/shard_map/all_gather | solution.py:45
  11.2 22.3 %all-to-all-start = ((bf16[8,128,512]{1,2,0:T(8,128)(2,1)}), bf16[8,128,512]{1,2,0:T(8,128)(2,1)S(1)}, u32[]{:S(2)}, u32[]{:S(2)}) async-start(bf16[8,128,512]{1,2,0:T(8,128)(2,1)} %stack.27), calls=%async_computation.1 | async-start | bytes 2097152 | tf_op jit(solution)/shard_map/all_to_all | solution.py:47
  15.5 213.9 %all-reduce.3.cloned.1.call-start = ((), (), s32[]{:S(2)}) async-start(), calls=%async_computation.6 | async-start | bytes 6291456
  33.5 3.3 %copy-start.2 = (bf16[1,32,128,128]{3,2,1,0:T(8,128)(2,1)S(1)}, bf16[1,32,128,128]{3,2,1,0:T(8,128)(2,1)}, u32[]{:S(2)}) copy-start(bf16[1,32,128,128]{3,2,1,0:T(8,128)(2,1)} %param.19) | copy-start | bytes 3145732
  36.8 1.0 copy-start.4
  42.8 3.4 %copy-start.1 = (bf16[1,32,128,128]{3,2,1,0:T(8,128)(2,1)S(1)}, bf16[1,32,128,128]{3,2,1,0:T(8,128)(2,1)}, u32[]{:S(2)}) copy-start(bf16[1,32,128,128]{3,2,1,0:T(8,128)(2,1)} %param.15) | copy-start | bytes 3145732
  48.0 2.3 copy-start.7
  50.8 2.3 copy-start.8
  65.6 2.4 copy-start.9
  65.6 2.4 copy-start.10
  70.0 2.4 copy-start.6
  70.0 196.0 %reduce-scatter.8.cloned.1.call-start = ((), (), s32[]{:S(2)}) async-start(), calls=%async_computation.5 | async-start | bytes 1179648 | tf_op jit(solution)/shard_map/reduce_scatter | solution.py:106
  79.5 1.5 copy-start.3
  79.5 1.9 copy-start.5
  81.0 221.7 %reduce-scatter.6.cloned.1.call-start = ((), (), s32[]{:S(2)}) async-start(), calls=%async_computation.4 | async-start | bytes 1179648 | tf_op jit(solution)/shard_map/reduce_scatter | solution.py:74
  84.9 1.6 copy-start.14
Sparse Core Ops, SparseCore 0:
  10.5 30.0 all-gather.1
  70.2 159.2 all-reduce.2
  232.5 33.5 reduce-scatter.7
  269.0 33.5 reduce-scatter.5
